TPU v7x, 1024 devices: a whole 4x4x32 slice. The times are simulated.
1024 devices in a mesh: rows: 64 (over z, core), dp: 16 (over x, y).
Axes of the slice: x: 4, y: 4, z: 32, core: 2. Of those that a mesh axis runs over, the one named last changes fastest.
Arguments:
- features: bfloat16 [48, 3456, 2048], P('dp', 'rows'), may hold values from -6 to 6
- depth_weight: bfloat16 [9, 2048], P(None, 'rows'), may hold values from -2 to 2
- point_weight: bfloat16 [2048, 256], replicated, may hold values from -0.125 to 0.125
- cotangent: bfloat16 [48, 3456, 256], P('dp', 'rows'), may hold values from -6 to 6
Outputs:
- branch_out: bfloat16 [48, 3456, 256], P('dp', 'rows')
- grad_features: bfloat16 [48, 3456, 2048], P('dp', None, 'rows')
- grad_point: float32 [2048, 256], P('rows')
- grad_depth: float32 [9, 2048], P(None, 'rows')
All inputs are finite; a program needn't handle non-finite values.
Results may differ from a plain program's by a relative error of at most 0.0061.
Values may be sent and summed in bfloat16 or wider, within the bound.
No kernel may reach another device: no remote copies, remote signals or barrier semaphores. Data moves between devices by JAX's collectives and lax.ppermute only.
A program may use at most 32 MiB of HBM per device.

v0:
```python
import math

import jax
import jax.numpy as jnp
from jax import lax
from jax.sharding import PartitionSpec as P

K = 256
DILATION_STEP = 12
H16 = 48
W16 = 72


def gelu_tanh(value):
    return jax.nn.gelu(value, approximate=True)


def padded_flat(flat_grid):
    reach = DILATION_STEP * W16 + DILATION_STEP
    return jnp.pad(flat_grid, ((0, 0), (0, 0), (reach, reach)))


def shifted(padded_grid, pixels, row_offset, column_offset):
    reach = DILATION_STEP * W16 + DILATION_STEP
    start = reach + DILATION_STEP * (row_offset * W16 + column_offset)
    view = padded_grid[:, :, start : start + pixels].astype(jnp.float32)
    column = jnp.arange(pixels, dtype=jnp.int32) % W16 + DILATION_STEP * column_offset
    keep = jnp.logical_and(column >= 0, column < W16)
    return jnp.where(keep, view, 0.0)


def depthwise(flat_grid, kernel, sign):
    pixels = flat_grid.shape[2]
    padded_grid = padded_flat(flat_grid)
    total = jnp.zeros(flat_grid.shape, jnp.float32)
    for row_offset in range(-1, 2):
        for column_offset in range(-1, 2):
            index = 3 * (row_offset + 1) + (column_offset + 1)
            view = shifted(padded_grid, pixels, sign * row_offset, sign * column_offset)
            total = total + view * kernel[index].astype(jnp.float32)[:, None]
    return total


def tap_sums(grad_mixed, flat_grid):
    pixels = flat_grid.shape[2]
    padded_grid = padded_flat(flat_grid)
    upstream = grad_mixed.astype(jnp.float32)
    rows_out = []
    for row_offset in range(-1, 2):
        for column_offset in range(-1, 2):
            view = shifted(padded_grid, pixels, row_offset, column_offset)
            rows_out.append(jnp.sum(upstream * view, axis=(0, 2)))
    return jnp.stack(rows_out, axis=0)


def on_device(features, depth_weight, point_weight, cotangent):
    local_chan = jnp.transpose(features, (0, 2, 1))
    chan_field = lax.all_to_all(local_chan, "rows", split_axis=1, concat_axis=2, tiled=True)
    samples, slice_width, pixels = chan_field.shape
    chan_mixed = depthwise(chan_field, depth_weight, 1).astype(jnp.bfloat16)
    row_mixed = lax.all_to_all(chan_mixed, "rows", split_axis=2, concat_axis=1, tiled=True)
    chans = row_mixed.shape[1]
    here = row_mixed.shape[2]
    flat = jnp.transpose(row_mixed, (0, 2, 1)).reshape(-1, chans)
    pre = jnp.dot(flat, point_weight, preferred_element_type=jnp.float32)
    act, pull = jax.vjp(gelu_tanh, pre)
    branch_out = act.astype(jnp.bfloat16).reshape(samples, here, K)
    grad_pre = pull(cotangent.reshape(-1, K).astype(jnp.float32))[0].astype(jnp.bfloat16)
    grad_rows = lax.dot_general(
        grad_pre, point_weight, (((1,), (1,)), ((), ())), preferred_element_type=jnp.float32
    )
    grad_rows = jnp.transpose(
        grad_rows.astype(jnp.bfloat16).reshape(samples, here, chans), (0, 2, 1)
    )
    point_part = lax.dot_general(
        flat, grad_pre, (((0,), (0,)), ((), ())), preferred_element_type=jnp.float32
    )
    grad_chan = lax.all_to_all(grad_rows, "rows", split_axis=1, concat_axis=2, tiled=True)
    grad_field = depthwise(grad_chan, depth_weight, -1).astype(jnp.bfloat16)
    grad_features = jnp.transpose(grad_field, (0, 2, 1))
    depth_part = tap_sums(grad_chan, chan_field)
    point_slice = lax.psum_scatter(point_part, "rows", scatter_dimension=0, tiled=True)
    grad_point, grad_depth = lax.psum((point_slice, depth_part), "dp")
    scale = 1.0 / math.sqrt(samples * lax.axis_size("dp") * H16 * W16)
    return (branch_out, grad_features, grad_point * scale, grad_depth * scale)


def solution(mesh):
    placed = (P("dp", "rows", None), P(None, "rows"), P(), P("dp", "rows", None))
    return jax.shard_map(
        on_device,
        mesh=mesh,
        in_specs=placed,
        out_specs=(P("dp", "rows", None), P("dp", None, "rows"), P("rows", None), P(None, "rows")),
        check_vma=False,
    )
```

profile of v0, /device:TPU:128, one launch (start us, length us, event | category | flops | bytes accessed | tf_op | source)
XLA Modules:
  0.0 590.3 jit_solution(2914428103313010899)
XLA Ops:
  7.2 0.0 copy-start
  7.2 4.1 copy.16
  11.3 3.0 bitcast_bitcast_fusion.1
  14.3 5.8 reshape.98
  20.1 27.8 %all-to-all-start = ((bf16[64,2,2592]{2,1,0:T(2,128)(2,1)}), bf16[64,2,2592]{2,1,0:T(2,128)(2,1)S(1)}, u32[]{:S(2)}, u32[]{:S(2)}) async-start(bf16[64,2,2592]{2,1,0:T(2,128)(2,1)} %reshape.98), calls=%async_computation | async-start | bytes 1376256 | tf_op jit(solution)/shard_map/all_to_all | solution.py:58
  48.0 0.0 copy-start.21
  48.0 0.0 copy-start.23
  48.0 62.9 %all-to-all-done = bf16[64,2,2592]{2,1,0:T(2,128)(2,1)S(1)} async-done(((bf16[64,2,2592]{2,1,0:T(2,128)(2,1)}), bf16[64,2,2592]{2,1,0:T(2,128)(2,1)S(1)}, u32[]{:S(2)}, u32[]{:S(2)}) %all-to-all-start) | async-done | bytes 663584 | tf_op jit(solution)/shard_map/all_to_all | solution.py:58
  110.9 5.9 reshape.99
  116.8 1.8 copy.17
  118.6 1.8 copy.18
  120.4 3.0 all_to_all.42
  123.5 3.3 add_convert_fusion
  126.7 5.3 copy.19
  132.1 7.0 %reshape.100 = bf16[64,2,2592]{2,1,0:T(2,128)(2,1)} reshape(bf16[3456,3,32]{2,1,0:T(4,128)(2,1)} %bitcast.78) | data formatting | bytes 1327104
  139.1 21.3 %all-to-all-start.1 = ((bf16[64,2,2592]{2,1,0:T(2,128)(2,1)}), bf16[64,2,2592]{2,1,0:T(2,128)(2,1)}, u32[]{:S(2)}, u32[]{:S(2)}) async-start(bf16[64,2,2592]{2,1,0:T(2,128)(2,1)} %reshape.100), calls=%async_computation.1 | async-start | bytes 1376256 | tf_op jit(solution)/shard_map/all_to_all | solution.py:61
  160.4 63.4 %all-to-all-done.1 = bf16[64,2,2592]{2,1,0:T(2,128)(2,1)} async-done(((bf16[64,2,2592]{2,1,0:T(2,128)(2,1)}), bf16[64,2,2592]{2,1,0:T(2,128)(2,1)}, u32[]{:S(2)}, u32[]{:S(2)}) %all-to-all-start.1) | async-done | bytes 663584 | tf_op jit(solution)/shard_map/all_to_all | solution.py:61
  223.8 7.3 %reshape.101 = bf16[3456,3,32]{2,1,0:T(4,128)(2,1)} reshape(bf16[64,2,2592]{2,1,0:T(2,128)(2,1)} %all-to-all-done.1) | data formatting | bytes 1327104
  231.1 5.8 copy.27
  236.9 2.5 copy.22
  239.4 2.2 reshape.85
  241.6 2.2 fusion.22
  243.8 1.4 convolution_convert_fusion
  245.1 2.1 reshape.87
  247.3 4.0 copy.23
  251.3 3.0 bitcast_bitcast_fusion
  254.3 5.8 reshape.102
  260.1 21.7 %all-to-all-start.2 = ((bf16[64,2,2592]{2,1,0:T(2,128)(2,1)}), bf16[64,2,2592]{2,1,0:T(2,128)(2,1)}, u32[]{:S(2)}, u32[]{:S(2)}) async-start(bf16[64,2,2592]{2,1,0:T(2,128)(2,1)} %reshape.102), calls=%async_computation.2 | async-start | bytes 1376256 | tf_op jit(solution)/shard_map/all_to_all | solution.py:78
  281.8 0.3 reduce-scatter.2.cloned.1.call-start
  282.1 3.0 fusion.43
  285.0 0.0 reduce-scatter.2.cloned.1.call-update
  285.1 0.8 copy-done.5
  285.9 0.7 reshape.86
  286.6 59.9 %all-to-all-done.2 = bf16[64,2,2592]{2,1,0:T(2,128)(2,1)} async-done(((bf16[64,2,2592]{2,1,0:T(2,128)(2,1)}), bf16[64,2,2592]{2,1,0:T(2,128)(2,1)}, u32[]{:S(2)}, u32[]{:S(2)}) %all-to-all-start.2) | async-done | bytes 663584 | tf_op jit(solution)/shard_map/all_to_all | solution.py:78
  346.5 7.5 %reshape.103 = bf16[2048,3,54]{2,1,0:T(4,128)(2,1)} reshape(bf16[64,2,2592]{2,1,0:T(2,128)(2,1)} %all-to-all-done.2) | data formatting | bytes 1327104
  354.0 1.8 copy.24
  355.8 1.1 copy-done.1
  357.0 1.8 copy.25
  358.7 3.8 all_to_all.50
  362.5 2.3 multiply_reduce_fusion
  364.8 0.0 copy-start.3
  364.9 0.0 copy-start.24
  364.9 2.7 fusion.14
  367.7 3.3 fusion.15
  371.0 137.0 %reduce-scatter.2.cloned.1.call-done = f32[32,256]{1,0:T(8,128)} async-done(((f32[2048,256]{1,0:T(8,128)}), f32[32,256]{1,0:T(8,128)}) %reduce-scatter.2.cloned.1.call-update) | async-done | bytes 32784 | tf_op jit(solution)/shard_map/reduce_scatter | solution.py:82
  508.0 74.2 %all-reduce.2 = (f32[32,256]{1,0:T(8,128)S(1)}, f32[9,32]{1,0:T(8,128)S(1)}) all-reduce(f32[32,256]{1,0:T(8,128)} %reduce-scatter.2.cloned.1.call-done, f32[9,32]{1,0:T(8,128)S(1)} %stack.39), channel_id=1, replica_groups=mesh['rows'=64,'dp'=16] {'dp'}, use_global_device_ids=true, to_apply=%region_1.2 | all-reduce | flops 8480 | bytes 67840 | tf_op jit(solution)/shard_map/psum | solution.py:83
  582.3 0.6 broadcast_multiply_fusion
  582.9 0.6 broadcast_multiply_fusion.1
  (49 shorter events, 0.2 us)
Async XLA Ops:
  7.2 234.4 %copy-start = (bf16[2048,256]{1,0:T(8,128)(2,1)S(1)}, bf16[2048,256]{1,0:T(8,128)(2,1)}, u32[]{:S(2)}) copy-start(bf16[2048,256]{1,0:T(8,128)(2,1)} %param.6) | copy-start | bytes 3145732
  20.1 27.8 %copy-start.6 = (bf16[9,32]{1,0:T(8,128)(2,1)S(1)}, bf16[9,32]{1,0:T(8,128)(2,1)}, u32[]{:S(2)}) copy-start(bf16[9,32]{1,0:T(8,128)(2,1)} %param.5) | copy-start | bytes 1732
  20.1 90.8 %all-to-all-start = ((bf16[64,2,2592]{2,1,0:T(2,128)(2,1)}), bf16[64,2,2592]{2,1,0:T(2,128)(2,1)S(1)}, u32[]{:S(2)}, u32[]{:S(2)}) async-start(bf16[64,2,2592]{2,1,0:T(2,128)(2,1)} %reshape.98), calls=%async_computation | async-start | bytes 1376256 | tf_op jit(solution)/shard_map/all_to_all | solution.py:58
  47.9 75.5 %copy-start.7 = (f32[32]{0:T(128)}, f32[32]{0:T(128)S(1)}, u32[]{:S(2)}) copy-start(f32[32]{0:T(128)S(1)} %get-tuple-element.21) | copy-start | bytes 388
  47.9 75.5 %copy-start.9 = (f32[32]{0:T(128)}, f32[32]{0:T(128)S(1)}, u32[]{:S(2)}) copy-start(f32[32]{0:T(128)S(1)} %get-tuple-element.22) | copy-start | bytes 388
  48.0 75.5 %copy-start.11 = (f32[32]{0:T(128)}, f32[32]{0:T(128)S(1)}, u32[]{:S(2)}) copy-start(f32[32]{0:T(128)S(1)} %get-tuple-element.23) | copy-start | bytes 388
  48.0 75.5 %copy-start.13 = (f32[32]{0:T(128)}, f32[32]{0:T(128)S(1)}, u32[]{:S(2)}) copy-start(f32[32]{0:T(128)S(1)} %get-tuple-element.24) | copy-start | bytes 388
  48.0 75.5 %copy-start.15 = (f32[32]{0:T(128)}, f32[32]{0:T(128)S(1)}, u32[]{:S(2)}) copy-start(f32[32]{0:T(128)S(1)} %get-tuple-element.25) | copy-start | bytes 388
  48.0 75.5 %copy-start.17 = (f32[32]{0:T(128)}, f32[32]{0:T(128)S(1)}, u32[]{:S(2)}) copy-start(f32[32]{0:T(128)S(1)} %get-tuple-element.26) | copy-start | bytes 388
  48.0 75.5 %copy-start.19 = (f32[32]{0:T(128)}, f32[32]{0:T(128)S(1)}, u32[]{:S(2)}) copy-start(f32[32]{0:T(128)S(1)} %get-tuple-element.27) | copy-start | bytes 388
  48.0 75.5 %copy-start.21 = (f32[32]{0:T(128)}, f32[32]{0:T(128)S(1)}, u32[]{:S(2)}) copy-start(f32[32]{0:T(128)S(1)} %get-tuple-element.28) | copy-start | bytes 388
  48.0 75.5 %copy-start.23 = (f32[32]{0:T(128)}, f32[32]{0:T(128)S(1)}, u32[]{:S(2)}) copy-start(f32[32]{0:T(128)S(1)} %get-tuple-element.29) | copy-start | bytes 388
  139.1 21.3 %copy-start.4 = (bf16[3,54,256]{2,1,0:T(8,128)(2,1)S(1)}, bf16[3,54,256]{2,1,0:T(8,128)(2,1)}, u32[]{:S(2)}) copy-start(bf16[3,54,256]{2,1,0:T(8,128)(2,1)} %param.7) | copy-start | bytes 248836
  139.1 84.7 %all-to-all-start.1 = ((bf16[64,2,2592]{2,1,0:T(2,128)(2,1)}), bf16[64,2,2592]{2,1,0:T(2,128)(2,1)}, u32[]{:S(2)}, u32[]{:S(2)}) async-start(bf16[64,2,2592]{2,1,0:T(2,128)(2,1)} %reshape.100), calls=%async_computation.1 | async-start | bytes 1376256 | tf_op jit(solution)/shard_map/all_to_all | solution.py:61
  260.1 86.5 %all-to-all-start.2 = ((bf16[64,2,2592]{2,1,0:T(2,128)(2,1)}), bf16[64,2,2592]{2,1,0:T(2,128)(2,1)}, u32[]{:S(2)}, u32[]{:S(2)}) async-start(bf16[64,2,2592]{2,1,0:T(2,128)(2,1)} %reshape.102), calls=%async_computation.2 | async-start | bytes 1376256 | tf_op jit(solution)/shard_map/all_to_all | solution.py:78
  281.8 226.2 %reduce-scatter.2.cloned.1.call-start = ((), (), s32[]{:S(2)}) async-start(), calls=%async_computation.4 | async-start | bytes 2129920 | tf_op jit(solution)/shard_map/reduce_scatter | solution.py:82
  285.0 0.9 copy-start.5
  355.8 1.2 copy-start.1
  362.5 2.3 copy-start.2
  364.8 2.8 copy-start.3
  364.8 2.8 copy-start.8
  364.8 2.8 copy-start.10
  364.8 2.8 copy-start.12
  364.8 2.8 copy-start.14
  364.8 2.8 copy-start.16
  364.9 2.8 copy-start.18
  364.9 2.8 copy-start.20
  364.9 2.8 copy-start.22
  364.9 2.8 copy-start.24
Sparse Core Ops, SparseCore 0:
  286.0 221.9 reduce-scatter.1
where the time goes:
time: 592 us; the launch traced here: 590 us
  waiting for transfers between devices  323 us (55%)
  local copies, waits for them, and re-layouts  88 us (15%)
  blocking collectives  74.2 us (13%)
  starting transfers between devices  71.1 us (12%)
  between operations  14.5 us (2%)
  other arithmetic  12.8 us (2%)
  matrix products  6.51 us (1%)
    reduce_scatter x1, waiting for transfers between devices, on_device(): lax.psum_scatter(point_part, 'rows', scatter_dimension=0, tiled=True)  137 us
    psum x1, blocking collectives, on_device(): grad_point, grad_depth = lax.psum((point_slice, depth_part), 'dp')  74.2 us
    all_to_all x1, waiting for transfers between devices, on_device(): lax.all_to_all(chan_mixed, 'rows', split_axis=2, concat_axis=1, tiled=True)  63.4 us
    all_to_all x1, waiting for transfers between devices, on_device(): lax.all_to_all(local_chan, 'rows', split_axis=1, concat_axis=2, tiled=True)  62.9 us
    all_to_all x1, waiting for transfers between devices, on_device(): lax.all_to_all(grad_rows, 'rows', split_axis=1, concat_axis=2, tiled=True)  59.9 us
    unnamed x59, local copies, waits for them, and re-layouts  51.4 us
    all_to_all x1, starting transfers between devices, on_device(): lax.all_to_all(local_chan, 'rows', split_axis=1, concat_axis=2, tiled=True)  27.8 us
    all_to_all x1, starting transfers between devices, on_device(): lax.all_to_all(grad_rows, 'rows', split_axis=1, concat_axis=2, tiled=True)  21.7 us
  transfers between devices with their start and end apart: 4, of which 4 were waited for; matrix products, arithmetic and copies ran while one was open for 4% of the time, Pallas kernels for 0%

commit v1 on v0

--- a/solution.py
+++ b/solution.py
@@ -66,20 +66,19 @@
     act, pull = jax.vjp(gelu_tanh, pre)
     branch_out = act.astype(jnp.bfloat16).reshape(samples, here, K)
     grad_pre = pull(cotangent.reshape(-1, K).astype(jnp.float32))[0].astype(jnp.bfloat16)
-    grad_rows = lax.dot_general(
-        grad_pre, point_weight, (((1,), (1,)), ((), ())), preferred_element_type=jnp.float32
+    grad_pre_all = lax.all_gather(grad_pre.reshape(samples, here, K), "rows", axis=1, tiled=True)
+    start = lax.axis_index("rows") * slice_width
+    weight_own = lax.dynamic_slice_in_dim(point_weight, start, slice_width, axis=0)
+    grad_chan = lax.dot_general(
+        weight_own, grad_pre_all, (((1,), (2,)), ((), ())), preferred_element_type=jnp.float32
     )
-    grad_rows = jnp.transpose(
-        grad_rows.astype(jnp.bfloat16).reshape(samples, here, chans), (0, 2, 1)
+    grad_chan = jnp.transpose(grad_chan, (1, 0, 2)).astype(jnp.bfloat16)
+    point_slice = lax.dot_general(
+        chan_mixed, grad_pre_all, (((0, 2), (0, 1)), ((), ())), preferred_element_type=jnp.float32
     )
-    point_part = lax.dot_general(
-        flat, grad_pre, (((0,), (0,)), ((), ())), preferred_element_type=jnp.float32
-    )
-    grad_chan = lax.all_to_all(grad_rows, "rows", split_axis=1, concat_axis=2, tiled=True)
     grad_field = depthwise(grad_chan, depth_weight, -1).astype(jnp.bfloat16)
     grad_features = jnp.transpose(grad_field, (0, 2, 1))
     depth_part = tap_sums(grad_chan, chan_field)
-    point_slice = lax.psum_scatter(point_part, "rows", scatter_dimension=0, tiled=True)
     grad_point, grad_depth = lax.psum((point_slice, depth_part), "dp")
     scale = 1.0 / math.sqrt(samples * lax.axis_size("dp") * H16 * W16)
     return (branch_out, grad_features, grad_point * scale, grad_depth * scale)

time: 592 us -> 464 us (0.78)
  the two profiles are of different devices: /device:TPU:128 before, /device:TPU:32 now
where the time goes in v1:
time: 464 us; the launch traced here: 463 us
  waiting for transfers between devices  280 us (60%)
  blocking collectives  74.4 us (16%)
  local copies, waits for them, and re-layouts  42.3 us (9%)
  starting transfers between devices  34.2 us (7%)
  between operations  14.2 us (3%)
  matrix products  10.7 us (2%)
  other arithmetic  7.07 us (2%)
    all_gather x1, waiting for transfers between devices, on_device(): lax.all_gather(grad_pre.reshape(samples, here, K), 'rows', axis=1, tiled=...  123 us
    all_to_all x1, waiting for transfers between devices, on_device(): lax.all_to_all(local_chan, 'rows', split_axis=1, concat_axis=2, tiled=True)  78.7 us
    all_to_all x1, waiting for transfers between devices, on_device(): lax.all_to_all(chan_mixed, 'rows', split_axis=2, concat_axis=1, tiled=True)  78.7 us
    psum x1, blocking collectives, on_device(): grad_point, grad_depth = lax.psum((point_slice, depth_part), 'dp')  74.4 us
    all_to_all x1, starting transfers between devices, on_device(): lax.all_to_all(local_chan, 'rows', split_axis=1, concat_axis=2, tiled=True)  29.3 us
    unnamed x20, local copies, waits for them, and re-layouts  28.3 us
  transfers between devices with their start and end apart: 3, of which 3 were waited for; matrix products, arithmetic and copies ran while one was open for 0% of the time, Pallas kernels for 0%

profile of v1, /device:TPU:32, one launch (start us, length us, event | category | flops | bytes accessed | tf_op | source)
XLA Modules:
  0.0 463.0 jit_solution(17380160271934883910)
XLA Ops:
  7.2 0.0 copy-start
  7.2 4.1 copy.13
  11.3 2.0 bitcast_bitcast_fusion
  13.3 4.3 reshape.98
  17.6 0.0 copy-start.6
  17.6 29.3 %all-to-all-start = ((bf16[64,2,2592]{2,1,0:T(2,128)(2,1)}), bf16[64,2,2592]{2,1,0:T(2,128)(2,1)}, u32[]{:S(2)}, u32[]{:S(2)}) async-start(bf16[64,2,2592]{2,1,0:T(2,128)(2,1)} %reshape.98), calls=%async_computation | async-start | bytes 1376256 | tf_op jit(solution)/shard_map/all_to_all | solution.py:58
  47.0 0.0 copy-done.6
  47.0 78.7 %all-to-all-done = bf16[64,2,2592]{2,1,0:T(2,128)(2,1)} async-done(((bf16[64,2,2592]{2,1,0:T(2,128)(2,1)}), bf16[64,2,2592]{2,1,0:T(2,128)(2,1)}, u32[]{:S(2)}, u32[]{:S(2)}) %all-to-all-start) | async-done | bytes 663584 | tf_op jit(solution)/shard_map/all_to_all | solution.py:58
  125.7 6.8 %reshape.99 = bf16[2048,3,54]{2,1,0:T(4,128)(2,1)S(1)} reshape(bf16[64,2,2592]{2,1,0:T(2,128)(2,1)} %all-to-all-done) | data formatting | bytes 1327104
  132.5 0.2 copy.14
  132.7 0.6 copy.15
  133.3 2.1 all_to_all.29
  135.4 0.0 copy-start.1
  135.4 2.5 add_convert_fusion
  137.9 0.0 copy-start.3
  138.0 3.8 copy.16
  141.8 0.0 copy-done.1
  141.8 0.0 copy-done.3
  141.8 7.0 %reshape.100 = bf16[64,2,2592]{2,1,0:T(2,128)(2,1)} reshape(bf16[3456,3,32]{2,1,0:T(4,128)(2,1)} %bitcast.70) | data formatting | bytes 1327104
  148.8 0.0 copy-start.5
  148.8 4.7 %all-to-all-start.1 = ((bf16[64,2,2592]{2,1,0:T(2,128)(2,1)}), bf16[64,2,2592]{2,1,0:T(2,128)(2,1)S(1)}, u32[]{:S(2)}, u32[]{:S(2)}) async-start(bf16[64,2,2592]{2,1,0:T(2,128)(2,1)} %reshape.100), calls=%async_computation.1 | async-start | bytes 1376256 | tf_op jit(solution)/shard_map/all_to_all | solution.py:61
  153.5 0.2 all-gather.2.cloned.1.call-start
  153.8 0.0 copy-done.5
  153.8 78.7 %all-to-all-done.1 = bf16[64,2,2592]{2,1,0:T(2,128)(2,1)S(1)} async-done(((bf16[64,2,2592]{2,1,0:T(2,128)(2,1)}), bf16[64,2,2592]{2,1,0:T(2,128)(2,1)S(1)}, u32[]{:S(2)}, u32[]{:S(2)}) %all-to-all-start.1) | async-done | bytes 663584 | tf_op jit(solution)/shard_map/all_to_all | solution.py:61
  232.5 4.0 reshape.101
  236.5 4.9 %copy.24 = bf16[3,32,64,54]{3,1,2,0:T(8,128)(2,1)S(1)} copy(bf16[3,32,64,54]{1,0,3,2:T(4,128)(2,1)} %bitcast.69) | data formatting | bytes 1327104 | tf_op jit(solution)/shard_map/all_to_all | solution.py:61
  241.4 0.8 copy.19
  242.2 0.2 reshape.83
  242.3 0.0 copy-done
  242.3 0.0 copy-start.2
  242.4 0.5 fusion.30
  242.9 0.7 copy.20
  243.6 0.0 all-gather.2.cloned.1.call-update
  243.6 0.7 reshape.84
  244.2 0.0 copy-start.4
  244.2 122.7 %all-gather.2.cloned.1.call-done = bf16[3,3456,256]{2,0,1:T(4,128)(2,1)} async-done(((bf16[3,54,256]{2,0,1:T(4,128)(2,1)}), bf16[3,3456,256]{2,0,1:T(4,128)(2,1)}) %all-gather.2.cloned.1.call-update) | async-done | bytes 5308432 | tf_op jit(solution)/shard_map/all_gather | solution.py:69
  366.9 0.0 copy-done.2
  366.9 6.2 %fusion.19 = (f32[32]{0:T(128)S(1)}, f32[32]{0:T(128)S(1)}, f32[32]{0:T(128)S(1)}, f32[32]{0:T(128)S(1)}, f32[32]{0:T(128)S(1)}, /*index=5*/f32[32]{0:T(128)S(1)...) fusion(pred[3456]{0:T(1024)(128)(4,1)S(1)} %get-tuple-element.33, ...), kind=kOutput, calls=%fused_computation.46 | convolution fusion | flops 182476512 | bytes 6665348 | tf_op jit(solution)/shard_map/dot_general | solution.py:72
  373.2 0.0 copy-done.4
  373.2 4.0 fusion.20
  377.2 74.4 %all-reduce.2 = (f32[32,256]{1,0:T(8,128)S(1)}, f32[9,32]{1,0:T(8,128)S(1)}) all-reduce(f32[32,256]{1,0:T(8,128)S(1)} %fusion.20, f32[9,32]{1,0:T(8,128)S(1)} %stack.39), channel_id=1, replica_groups=mesh['rows'=64,'dp'=16] {'dp'}, use_global_device_ids=true, to_apply=%region_0.1 | all-reduce | flops 8480 | bytes 67840 | tf_op jit(solution)/shard_map/psum | solution.py:82
  451.6 0.6 broadcast_multiply_fusion
  452.2 0.6 broadcast_multiply_fusion.1
  452.8 3.3 fusion.23
  (6 shorter events, 0.1 us)
Async XLA Ops:
  7.2 235.2 %copy-start = (bf16[2048,256]{1,0:T(8,128)(2,1)S(1)}, bf16[2048,256]{1,0:T(8,128)(2,1)}, u32[]{:S(2)}) copy-start(bf16[2048,256]{1,0:T(8,128)(2,1)} %param.6) | copy-start | bytes 3145732
  17.6 29.4 %copy-start.6 = (bf16[9,32]{1,0:T(8,128)(2,1)S(1)}, bf16[9,32]{1,0:T(8,128)(2,1)}, u32[]{:S(2)}) copy-start(bf16[9,32]{1,0:T(8,128)(2,1)} %param.5) | copy-start | bytes 1732
  17.6 108.1 %all-to-all-start = ((bf16[64,2,2592]{2,1,0:T(2,128)(2,1)}), bf16[64,2,2592]{2,1,0:T(2,128)(2,1)}, u32[]{:S(2)}, u32[]{:S(2)}) async-start(bf16[64,2,2592]{2,1,0:T(2,128)(2,1)} %reshape.98), calls=%async_computation | async-start | bytes 1376256 | tf_op jit(solution)/shard_map/all_to_all | solution.py:58
  135.4 6.4 %copy-start.1 = (bf16[3,32,3456]{2,1,0:T(8,128)(2,1)}, bf16[3,32,3456]{2,1,0:T(8,128)(2,1)S(1)}, u32[]{:S(2)}) copy-start(bf16[3,32,3456]{2,1,0:T(8,128)(2,1)S(1)} %all_to_all.29) | copy-start | bytes 1990660
  137.9 3.8 copy-start.3
  148.8 5.0 %copy-start.5 = (bf16[3,54,256]{2,1,0:T(8,128)(2,1)S(1)}, bf16[3,54,256]{2,1,0:T(8,128)(2,1)}, u32[]{:S(2)}) copy-start(bf16[3,54,256]{2,1,0:T(8,128)(2,1)} %param.7) | copy-start | bytes 248836
  148.8 83.7 %all-to-all-start.1 = ((bf16[64,2,2592]{2,1,0:T(2,128)(2,1)}), bf16[64,2,2592]{2,1,0:T(2,128)(2,1)S(1)}, u32[]{:S(2)}, u32[]{:S(2)}) async-start(bf16[64,2,2592]{2,1,0:T(2,128)(2,1)} %reshape.100), calls=%async_computation.1 | async-start | bytes 1376256 | tf_op jit(solution)/shard_map/all_to_all | solution.py:61
  153.5 213.4 %all-gather.2.cloned.1.call-start = ((), (), s32[]{:S(2)}) async-start(), calls=%async_computation.2 | async-start | bytes 7188480 | tf_op jit(solution)/shard_map/all_gather | solution.py:69
  242.3 124.6 %copy-start.2 = (bf16[3,32,3456]{2,1,0:T(8,128)(2,1)S(1)}, bf16[3,32,3456]{2,1,0:T(8,128)(2,1)}, u32[]{:S(2)}) copy-start(bf16[3,32,3456]{2,1,0:T(8,128)(2,1)} %copy-done.1) | copy-start | bytes 1990660
  244.2 128.9 %copy-start.4 = (bf16[3,32,3456]{2,1,0:T(8,128)(2,1)S(1)}, bf16[3,32,3456]{2,1,0:T(8,128)(2,1)}, u32[]{:S(2)}) copy-start(bf16[3,32,3456]{2,1,0:T(8,128)(2,1)} %copy-done.3) | copy-start | bytes 1990660
Sparse Core Ops, SparseCore 0:
  243.7 123.1 all-gather.1

commit v2 on v1

--- a/solution.py
+++ b/solution.py
@@ -79,7 +79,13 @@
     grad_field = depthwise(grad_chan, depth_weight, -1).astype(jnp.bfloat16)
     grad_features = jnp.transpose(grad_field, (0, 2, 1))
     depth_part = tap_sums(grad_chan, chan_field)
-    grad_point, grad_depth = lax.psum((point_slice, depth_part), "dp")
+    taps = depth_part.shape[0]
+    packed = jnp.concatenate(
+        [point_slice, jnp.pad(depth_part, ((0, 0), (0, K - depth_part.shape[1])))], axis=0
+    )
+    summed = lax.all_gather(packed, "dp", axis=0, tiled=False).sum(axis=0)
+    grad_point = summed[:slice_width]
+    grad_depth = summed[slice_width : slice_width + taps, : depth_part.shape[1]]
     scale = 1.0 / math.sqrt(samples * lax.axis_size("dp") * H16 * W16)
     return (branch_out, grad_features, grad_point * scale, grad_depth * scale)
 

time: 464 us -> 415 us (0.89)
  the two profiles are of different devices: /device:TPU:32 before, /device:TPU:4 now
where the time goes in v2:
time: 415 us
  waiting for transfers between devices  281 us (68%)
  local copies, waits for them, and re-layouts  42.3 us (10%)
  starting transfers between devices  34.7 us (8%)
  blocking collectives  24.1 us (6%)
  between operations  14.2 us (3%)
  matrix products  10.7 us (3%)
  other arithmetic  7.17 us (2%)
    all_gather x1, waiting for transfers between devices, on_device(): lax.all_gather(grad_pre.reshape(samples, here, K), 'rows', axis=1, tiled=...  123 us
    all_to_all x1, waiting for transfers between devices, on_device(): lax.all_to_all(chan_mixed, 'rows', split_axis=2, concat_axis=1, tiled=True)  79.6 us
    all_to_all x1, waiting for transfers between devices, on_device(): lax.all_to_all(local_chan, 'rows', split_axis=1, concat_axis=2, tiled=True)  78.7 us
    all_to_all x1, starting transfers between devices, on_device(): lax.all_to_all(local_chan, 'rows', split_axis=1, concat_axis=2, tiled=True)  29.7 us
    unnamed x20, local copies, waits for them, and re-layouts  28.3 us
    all_gather x1, blocking collectives, on_device(): summed = lax.all_gather(packed, 'dp', axis=0, tiled=False).sum(axis=0)  24.1 us
  transfers between devices with their start and end apart: 3, of which 3 were waited for; matrix products, arithmetic and copies ran while one was open for 0% of the time, Pallas kernels for 0%

profile of v2, /device:TPU:4, one launch (start us, length us, event | category | flops | bytes accessed | tf_op | source)
XLA Modules:
  0.0 414.7 jit_solution(4731645273489566631)
XLA Ops:
  7.2 0.0 copy-start
  7.2 4.1 copy.13
  11.3 2.0 bitcast_bitcast_fusion
  13.3 4.3 %reshape.102 = bf16[64,2,2592]{2,1,0:T(2,128)(2,1)} reshape(bf16[2048,3,54]{2,1,0:T(4,128)(2,1)S(1)} %bitcast_bitcast_fusion) | data formatting | bytes 1327104
  17.6 0.0 copy-start.6
  17.6 29.7 %all-to-all-start = ((bf16[64,2,2592]{2,1,0:T(2,128)(2,1)}), bf16[64,2,2592]{2,1,0:T(2,128)(2,1)}, u32[]{:S(2)}, u32[]{:S(2)}) async-start(bf16[64,2,2592]{2,1,0:T(2,128)(2,1)} %reshape.102), calls=%async_computation | async-start | bytes 1376256 | tf_op jit(solution)/shard_map/all_to_all | solution.py:58
  47.4 0.0 copy-done.6
  47.4 78.7 %all-to-all-done = bf16[64,2,2592]{2,1,0:T(2,128)(2,1)} async-done(((bf16[64,2,2592]{2,1,0:T(2,128)(2,1)}), bf16[64,2,2592]{2,1,0:T(2,128)(2,1)}, u32[]{:S(2)}, u32[]{:S(2)}) %all-to-all-start) | async-done | bytes 663584 | tf_op jit(solution)/shard_map/all_to_all | solution.py:58
  126.1 6.8 %reshape.103 = bf16[2048,3,54]{2,1,0:T(4,128)(2,1)S(1)} reshape(bf16[64,2,2592]{2,1,0:T(2,128)(2,1)} %all-to-all-done) | data formatting | bytes 1327104
  132.9 0.2 copy.14
  133.1 0.6 copy.15
  133.7 2.1 all_to_all.29
  135.8 0.0 copy-start.1
  135.8 2.5 add_convert_fusion
  138.3 0.0 copy-start.3
  138.4 3.8 copy.16
  142.2 0.0 copy-done.1
  142.2 0.0 copy-done.3
  142.2 7.0 %reshape.104 = bf16[64,2,2592]{2,1,0:T(2,128)(2,1)} reshape(bf16[3456,3,32]{2,1,0:T(4,128)(2,1)} %bitcast.72) | data formatting | bytes 1327104
  149.2 0.0 copy-start.5
  149.2 4.8 %all-to-all-start.1 = ((bf16[64,2,2592]{2,1,0:T(2,128)(2,1)}), bf16[64,2,2592]{2,1,0:T(2,128)(2,1)S(1)}, u32[]{:S(2)}, u32[]{:S(2)}) async-start(bf16[64,2,2592]{2,1,0:T(2,128)(2,1)} %reshape.104), calls=%async_computation.1 | async-start | bytes 1376256 | tf_op jit(solution)/shard_map/all_to_all | solution.py:61
  154.0 0.2 all-gather.4.cloned.1.call-start
  154.2 0.0 copy-done.5
  154.2 79.6 %all-to-all-done.1 = bf16[64,2,2592]{2,1,0:T(2,128)(2,1)S(1)} async-done(((bf16[64,2,2592]{2,1,0:T(2,128)(2,1)}), bf16[64,2,2592]{2,1,0:T(2,128)(2,1)S(1)}, u32[]{:S(2)}, u32[]{:S(2)}) %all-to-all-start.1) | async-done | bytes 663584 | tf_op jit(solution)/shard_map/all_to_all | solution.py:61
  233.8 4.0 reshape.105
  237.8 4.9 %copy.24 = bf16[3,32,64,54]{3,1,2,0:T(8,128)(2,1)S(1)} copy(bf16[3,32,64,54]{1,0,3,2:T(4,128)(2,1)} %bitcast.71) | data formatting | bytes 1327104 | tf_op jit(solution)/shard_map/all_to_all | solution.py:61
  242.7 0.8 copy.19
  243.5 0.2 reshape.83
  243.7 0.0 copy-done
  243.7 0.0 copy-start.2
  243.7 0.5 fusion.30
  244.2 0.7 copy.20
  244.9 0.0 all-gather.4.cloned.1.call-update
  244.9 0.7 reshape.84
  245.6 0.0 copy-start.4
  245.6 123.2 %all-gather.4.cloned.1.call-done = bf16[3,3456,256]{2,0,1:T(4,128)(2,1)} async-done(((bf16[3,54,256]{2,0,1:T(4,128)(2,1)}), bf16[3,3456,256]{2,0,1:T(4,128)(2,1)}) %all-gather.4.cloned.1.call-update) | async-done | bytes 5308432 | tf_op jit(solution)/shard_map/all_gather | solution.py:69
  368.8 0.0 copy-done.2
  368.8 6.2 %fusion.19 = (f32[32]{0:T(128)S(1)}, f32[32]{0:T(128)S(1)}, f32[32]{0:T(128)S(1)}, f32[32]{0:T(128)S(1)}, f32[32]{0:T(128)S(1)}, /*index=5*/f32[32]{0:T(128)S(1)...) fusion(pred[3456]{0:T(1024)(128)(4,1)S(1)} %get-tuple-element.31, ...), kind=kOutput, calls=%fused_computation.46 | convolution fusion | flops 182476512 | bytes 6665348 | tf_op jit(solution)/shard_map/dot_general | solution.py:72
  375.1 0.0 copy-done.4
  375.1 4.0 fusion.20
  379.1 24.1 %all-gather.1 = f32[16,41,256]{2,1,0:T(8,128)S(1)} all-gather(f32[1,41,256]{2,1,0:T(8,128)S(1)} %fusion.31), channel_id=2, replica_groups=mesh['rows'=64,'dp'=16] {'dp'}, dimensions={0}, use_global_device_ids=true | all-gather | bytes 713728 | tf_op jit(solution)/shard_map/all_gather | solution.py:86
  403.2 0.1 reduce_sum.99
  403.3 0.6 slice_multiply_fusion
  403.9 0.6 slice_multiply_fusion.1
  404.5 3.3 fusion.23
  (7 shorter events, 0.2 us)
Async XLA Ops:
  7.2 236.5 %copy-start = (bf16[2048,256]{1,0:T(8,128)(2,1)S(1)}, bf16[2048,256]{1,0:T(8,128)(2,1)}, u32[]{:S(2)}) copy-start(bf16[2048,256]{1,0:T(8,128)(2,1)} %param.6) | copy-start | bytes 3145732
  17.6 29.8 %copy-start.6 = (bf16[9,32]{1,0:T(8,128)(2,1)S(1)}, bf16[9,32]{1,0:T(8,128)(2,1)}, u32[]{:S(2)}) copy-start(bf16[9,32]{1,0:T(8,128)(2,1)} %param.5) | copy-start | bytes 1732
  17.6 108.5 %all-to-all-start = ((bf16[64,2,2592]{2,1,0:T(2,128)(2,1)}), bf16[64,2,2592]{2,1,0:T(2,128)(2,1)}, u32[]{:S(2)}, u32[]{:S(2)}) async-start(bf16[64,2,2592]{2,1,0:T(2,128)(2,1)} %reshape.102), calls=%async_computation | async-start | bytes 1376256 | tf_op jit(solution)/shard_map/all_to_all | solution.py:58
  135.8 6.4 %copy-start.1 = (bf16[3,32,3456]{2,1,0:T(8,128)(2,1)}, bf16[3,32,3456]{2,1,0:T(8,128)(2,1)S(1)}, u32[]{:S(2)}) copy-start(bf16[3,32,3456]{2,1,0:T(8,128)(2,1)S(1)} %all_to_all.29) | copy-start | bytes 1990660
  138.3 3.8 copy-start.3
  149.2 5.0 %copy-start.5 = (bf16[3,54,256]{2,1,0:T(8,128)(2,1)S(1)}, bf16[3,54,256]{2,1,0:T(8,128)(2,1)}, u32[]{:S(2)}) copy-start(bf16[3,54,256]{2,1,0:T(8,128)(2,1)} %param.7) | copy-start | bytes 248836
  149.2 84.6 %all-to-all-start.1 = ((bf16[64,2,2592]{2,1,0:T(2,128)(2,1)}), bf16[64,2,2592]{2,1,0:T(2,128)(2,1)S(1)}, u32[]{:S(2)}, u32[]{:S(2)}) async-start(bf16[64,2,2592]{2,1,0:T(2,128)(2,1)} %reshape.104), calls=%async_computation.1 | async-start | bytes 1376256 | tf_op jit(solution)/shard_map/all_to_all | solution.py:61
  154.0 214.8 %all-gather.4.cloned.1.call-start = ((), (), s32[]{:S(2)}) async-start(), calls=%async_computation.2 | async-start | bytes 7188480 | tf_op jit(solution)/shard_map/all_gather | solution.py:69
  243.7 125.1 %copy-start.2 = (bf16[3,32,3456]{2,1,0:T(8,128)(2,1)S(1)}, bf16[3,32,3456]{2,1,0:T(8,128)(2,1)}, u32[]{:S(2)}) copy-start(bf16[3,32,3456]{2,1,0:T(8,128)(2,1)} %copy-done.1) | copy-start | bytes 1990660
  245.6 129.5 %copy-start.4 = (bf16[3,32,3456]{2,1,0:T(8,128)(2,1)S(1)}, bf16[3,32,3456]{2,1,0:T(8,128)(2,1)}, u32[]{:S(2)}) copy-start(bf16[3,32,3456]{2,1,0:T(8,128)(2,1)} %copy-done.3) | copy-start | bytes 1990660
Sparse Core Ops, SparseCore 0:
  245.0 123.7 all-gather.3

commit v3 on v2

v3 whole, which is shorter than its diff:
```python
import math

import jax
import jax.numpy as jnp
from jax import lax
from jax.sharding import PartitionSpec as P

K = 256
DILATION_STEP = 12
H16 = 48
W16 = 72


def gelu_tanh(value):
    return jax.nn.gelu(value, approximate=True)


def padded_flat(flat_grid):
    reach = DILATION_STEP * W16 + DILATION_STEP
    return jnp.pad(flat_grid, ((0, 0), (reach, reach), (0, 0)))


def shifted(padded_grid, pixels, row_offset, column_offset):
    reach = DILATION_STEP * W16 + DILATION_STEP
    start = reach + DILATION_STEP * (row_offset * W16 + column_offset)
    view = padded_grid[:, start : start + pixels, :].astype(jnp.float32)
    column = jnp.arange(pixels, dtype=jnp.int32) % W16 + DILATION_STEP * column_offset
    keep = jnp.logical_and(column >= 0, column < W16)[:, None]
    return jnp.where(keep, view, 0.0)


def depthwise(flat_grid, kernel, sign):
    pixels = flat_grid.shape[1]
    padded_grid = padded_flat(flat_grid)
    total = jnp.zeros(flat_grid.shape, jnp.float32)
    for row_offset in range(-1, 2):
        for column_offset in range(-1, 2):
            index = 3 * (row_offset + 1) + (column_offset + 1)
            view = shifted(padded_grid, pixels, sign * row_offset, sign * column_offset)
            total = total + view * kernel[index].astype(jnp.float32)
    return total


def tap_sums(grad_mixed, flat_grid):
    pixels = flat_grid.shape[1]
    padded_grid = padded_flat(flat_grid)
    upstream = grad_mixed.astype(jnp.float32)
    rows_out = []
    for row_offset in range(-1, 2):
        for column_offset in range(-1, 2):
            view = shifted(padded_grid, pixels, row_offset, column_offset)
            rows_out.append(jnp.sum(upstream * view, axis=(0, 1)))
    return jnp.stack(rows_out, axis=0)


def on_device(features, depth_weight, point_weight, cotangent):
    samples, here, chans = features.shape
    parts = lax.axis_size("rows")
    slice_width = chans // parts
    blocks = jnp.transpose(features.reshape(samples, here, parts, slice_width), (2, 0, 1, 3))
    arrived = lax.all_to_all(blocks, "rows", split_axis=0, concat_axis=0, tiled=True)
    chan_field = jnp.transpose(arrived, (1, 0, 2, 3)).reshape(samples, parts * here, slice_width)
    chan_mixed = depthwise(chan_field, depth_weight, 1).astype(jnp.bfloat16)
    outgoing = jnp.transpose(chan_mixed.reshape(samples, parts, here, slice_width), (1, 0, 2, 3))
    returned = lax.all_to_all(outgoing, "rows", split_axis=0, concat_axis=0, tiled=True)
    row_mixed = jnp.transpose(returned, (1, 2, 0, 3)).reshape(samples * here, chans)
    pre = jnp.dot(row_mixed, point_weight, preferred_element_type=jnp.float32)
    act, pull = jax.vjp(gelu_tanh, pre)
    branch_out = act.astype(jnp.bfloat16).reshape(samples, here, K)
    grad_pre = pull(cotangent.reshape(-1, K).astype(jnp.float32))[0].astype(jnp.bfloat16)
    grad_pre_all = lax.all_gather(grad_pre.reshape(samples, here, K), "rows", axis=1, tiled=True)
    start = lax.axis_index("rows") * slice_width
    weight_own = lax.dynamic_slice_in_dim(point_weight, start, slice_width, axis=0)
    grad_chan = lax.dot_general(
        grad_pre_all, weight_own, (((2,), (1,)), ((), ())), preferred_element_type=jnp.float32
    ).astype(jnp.bfloat16)
    point_slice = lax.dot_general(
        chan_mixed, grad_pre_all, (((0, 1), (0, 1)), ((), ())), preferred_element_type=jnp.float32
    )
    grad_features = depthwise(grad_chan, depth_weight, -1).astype(jnp.bfloat16)
    depth_part = tap_sums(grad_chan, chan_field)
    taps = depth_part.shape[0]
    packed = jnp.concatenate(
        [point_slice, jnp.pad(depth_part, ((0, 0), (0, K - depth_part.shape[1])))], axis=0
    )
    summed = lax.all_gather(packed, "dp", axis=0, tiled=False).sum(axis=0)
    grad_point = summed[:slice_width]
    grad_depth = summed[slice_width : slice_width + taps, : depth_part.shape[1]]
    scale = 1.0 / math.sqrt(samples * lax.axis_size("dp") * H16 * W16)
    return (branch_out, grad_features, grad_point * scale, grad_depth * scale)


def solution(mesh):
    placed = (P("dp", "rows", None), P(None, "rows"), P(), P("dp", "rows", None))
    return jax.shard_map(
        on_device,
        mesh=mesh,
        in_specs=placed,
        out_specs=(P("dp", "rows", None), P("dp", None, "rows"), P("rows", None), P(None, "rows")),
        check_vma=False,
    )
```

time: 415 us -> 407 us (0.981)
  the two profiles are of different devices: /device:TPU:4 before, /device:TPU:2 now
where the time goes in v3:
time: 407 us
  waiting for transfers between devices  282 us (69%)
  starting transfers between devices  34.2 us (8%)
  local copies, waits for them, and re-layouts  33 us (8%)
  blocking collectives  24.1 us (6%)
  between operations  14.2 us (3%)
  matrix products  12.2 us (3%)
  other arithmetic  7.17 us (2%)
    all_gather x1, waiting for transfers between devices, on_device(): lax.all_gather(grad_pre.reshape(samples, here, K), 'rows', axis=1, tiled=...  123 us
    all_to_all x1, waiting for transfers between devices, on_device(): lax.all_to_all(outgoing, 'rows', split_axis=0, concat_axis=0, tiled=True)  79.7 us
    all_to_all x1, waiting for transfers between devices, on_device(): lax.all_to_all(blocks, 'rows', split_axis=0, concat_axis=0, tiled=True)  78.8 us
    all_to_all x1, starting transfers between devices, on_device(): lax.all_to_all(blocks, 'rows', split_axis=0, concat_axis=0, tiled=True)  29.4 us
    all_gather x1, blocking collectives, on_device(): summed = lax.all_gather(packed, 'dp', axis=0, tiled=False).sum(axis=0)  24.1 us
    unnamed x19, local copies, waits for them, and re-layouts  15.4 us
  transfers between devices with their start and end apart: 3, of which 3 were waited for; matrix products, arithmetic and copies ran while one was open for 0% of the time, Pallas kernels for 0%

profile of v3, /device:TPU:2, one launch (start us, length us, event | category | flops | bytes accessed | tf_op | source)
XLA Modules:
  0.0 406.7 jit_solution(3015016212865202279)
XLA Ops:
  7.2 0.0 copy-start
  7.2 2.6 copy.12
  9.8 1.7 copy.31
  11.5 0.0 copy-start.6
  11.5 3.2 reshape.114
  14.7 29.4 %all-to-all-start = ((bf16[64,2,2592]{2,1,0:T(2,128)(2,1)}), bf16[64,2,2592]{2,1,0:T(2,128)(2,1)S(1)}, u32[]{:S(2)}, u32[]{:S(2)}) async-start(bf16[64,2,2592]{2,1,0:T(2,128)(2,1)} %reshape.114), calls=%async_computation | async-start | bytes 1376256 | tf_op jit(solution)/shard_map/all_to_all | solution.py:61
  44.2 0.0 copy-done.6
  44.2 78.8 %all-to-all-done = bf16[64,2,2592]{2,1,0:T(2,128)(2,1)S(1)} async-done(((bf16[64,2,2592]{2,1,0:T(2,128)(2,1)}), bf16[64,2,2592]{2,1,0:T(2,128)(2,1)S(1)}, u32[]{:S(2)}, u32[]{:S(2)}) %all-to-all-start) | async-done | bytes 663584 | tf_op jit(solution)/shard_map/all_to_all | solution.py:61
  123.0 3.1 reshape.115
  126.1 0.3 bitcast_bitcast_fusion.1
  126.4 0.6 copy.14
  127.0 2.1 reshape.93
  129.1 0.0 copy-start.3
  129.1 2.5 add_convert_fusion
  131.6 0.0 copy-start.1
  131.6 5.6 %reshape.94 = bf16[3,64,54,32]{2,1,3,0:T(8,128)(2,1)} reshape(bf16[3,3456,32]{1,2,0:T(8,128)(2,1)S(1)} %add_convert_fusion) | data formatting | bytes 1327104 | tf_op jit(solution)/shard_map/reshape | solution.py:64
  137.2 0.0 copy-done.3
  137.2 0.0 copy-done.1
  137.2 2.4 copy.30
  139.7 0.0 copy-start.5
  139.7 3.2 reshape.116
  142.9 4.8 %all-to-all-start.1 = ((bf16[64,2,2592]{2,1,0:T(2,128)(2,1)}), bf16[64,2,2592]{2,1,0:T(2,128)(2,1)S(1)}, u32[]{:S(2)}, u32[]{:S(2)}) async-start(bf16[64,2,2592]{2,1,0:T(2,128)(2,1)} %reshape.116), calls=%async_computation.1 | async-start | bytes 1376256 | tf_op jit(solution)/shard_map/all_to_all | solution.py:65
  147.8 0.0 all-gather.4.cloned.1.call-start
  147.8 0.0 copy-done.5
  147.8 79.7 %all-to-all-done.1 = bf16[64,2,2592]{2,1,0:T(2,128)(2,1)S(1)} async-done(((bf16[64,2,2592]{2,1,0:T(2,128)(2,1)}), bf16[64,2,2592]{2,1,0:T(2,128)(2,1)S(1)}, u32[]{:S(2)}, u32[]{:S(2)}) %all-to-all-start.1) | async-done | bytes 663584 | tf_op jit(solution)/shard_map/all_to_all | solution.py:65
  227.6 3.1 reshape.117
  230.7 0.3 bitcast_bitcast_fusion
  231.0 1.1 copy.16
  232.0 2.2 reshape.95
  234.2 0.0 copy-done
  234.3 0.0 copy-start.4
  234.3 1.9 fusion.28
  236.2 0.7 copy.17
  236.9 0.0 all-gather.4.cloned.1.call-update
  236.9 0.7 reshape.96
  237.6 0.0 copy-start.2
  237.6 123.2 %all-gather.4.cloned.1.call-done = bf16[3,3456,256]{2,0,1:T(4,128)(2,1)} async-done(((bf16[3,54,256]{2,0,1:T(4,128)(2,1)}), bf16[3,3456,256]{2,0,1:T(4,128)(2,1)}) %all-gather.4.cloned.1.call-update) | async-done | bytes 5308432 | tf_op jit(solution)/shard_map/all_gather | solution.py:71
  360.8 0.0 copy-done.4
  360.8 6.3 %fusion.18 = (f32[32]{0:T(128)S(1)}, f32[32]{0:T(128)S(1)}, f32[32]{0:T(128)S(1)}, f32[32]{0:T(128)S(1)}, f32[32]{0:T(128)S(1)}, /*index=5*/f32[32]{0:T(128)S(1)...) fusion(pred[3456]{0:T(1024)(128)(4,1)S(1)} %get-tuple-element.31, ...), kind=kOutput, calls=%fused_computation.45 | convolution fusion | flops 182476512 | bytes 6665348 | tf_op jit(solution)/shard_map/dot_general | solution.py:74
  367.1 0.0 copy-done.2
  367.1 4.0 fusion.19
  371.2 24.1 %all-gather.1 = f32[16,41,256]{2,1,0:T(8,128)S(1)} all-gather(f32[1,41,256]{2,1,0:T(8,128)S(1)} %fusion.29), channel_id=2, replica_groups=mesh['rows'=64,'dp'=16] {'dp'}, dimensions={0}, use_global_device_ids=true | all-gather | bytes 713728 | tf_op jit(solution)/shard_map/all_gather | solution.py:86
  395.3 0.1 reduce_sum.99
  395.4 0.6 slice_multiply_fusion
  396.0 0.6 slice_multiply_fusion.1
  396.6 3.3 fusion.9
  (7 shorter events, 0.2 us)
Async XLA Ops:
  7.2 227.1 %copy-start = (bf16[2048,256]{1,0:T(8,128)(2,1)S(1)}, bf16[2048,256]{1,0:T(8,128)(2,1)}, u32[]{:S(2)}) copy-start(bf16[2048,256]{1,0:T(8,128)(2,1)} %param.6) | copy-start | bytes 3145732
  11.5 32.7 %copy-start.6 = (bf16[9,32]{1,0:T(8,128)(2,1)S(1)}, bf16[9,32]{1,0:T(8,128)(2,1)}, u32[]{:S(2)}) copy-start(bf16[9,32]{1,0:T(8,128)(2,1)} %param.5) | copy-start | bytes 1732
  14.7 108.2 %all-to-all-start = ((bf16[64,2,2592]{2,1,0:T(2,128)(2,1)}), bf16[64,2,2592]{2,1,0:T(2,128)(2,1)S(1)}, u32[]{:S(2)}, u32[]{:S(2)}) async-start(bf16[64,2,2592]{2,1,0:T(2,128)(2,1)} %reshape.114), calls=%async_computation | async-start | bytes 1376256 | tf_op jit(solution)/shard_map/all_to_all | solution.py:61
  129.1 8.1 %copy-start.3 = (bf16[3,3456,32]{1,2,0:T(8,128)(2,1)}, bf16[3,3456,32]{1,2,0:T(8,128)(2,1)S(1)}, u32[]{:S(2)}) copy-start(bf16[3,3456,32]{1,2,0:T(8,128)(2,1)S(1)} %reshape.93) | copy-start | bytes 1990660
  131.6 5.6 %copy-start.1 = (bf16[3,3456,32]{1,2,0:T(8,128)(2,1)}, bf16[3,3456,32]{1,2,0:T(8,128)(2,1)S(1)}, u32[]{:S(2)}) copy-start(bf16[3,3456,32]{1,2,0:T(8,128)(2,1)S(1)} %add_convert_fusion) | copy-start | bytes 1990660
  139.7 8.1 %copy-start.5 = (bf16[3,54,256]{2,1,0:T(8,128)(2,1)S(1)}, bf16[3,54,256]{2,1,0:T(8,128)(2,1)}, u32[]{:S(2)}) copy-start(bf16[3,54,256]{2,1,0:T(8,128)(2,1)} %param.7) | copy-start | bytes 248836
  142.9 84.6 %all-to-all-start.1 = ((bf16[64,2,2592]{2,1,0:T(2,128)(2,1)}), bf16[64,2,2592]{2,1,0:T(2,128)(2,1)S(1)}, u32[]{:S(2)}, u32[]{:S(2)}) async-start(bf16[64,2,2592]{2,1,0:T(2,128)(2,1)} %reshape.116), calls=%async_computation.1 | async-start | bytes 1376256 | tf_op jit(solution)/shard_map/all_to_all | solution.py:65
  147.8 213.0 %all-gather.4.cloned.1.call-start = ((), (), s32[]{:S(2)}) async-start(), calls=%async_computation.2 | async-start | bytes 7188480 | tf_op jit(solution)/shard_map/all_gather | solution.py:71
  234.3 126.5 %copy-start.4 = (bf16[3,3456,32]{1,2,0:T(8,128)(2,1)S(1)}, bf16[3,3456,32]{1,2,0:T(8,128)(2,1)}, u32[]{:S(2)}) copy-start(bf16[3,3456,32]{1,2,0:T(8,128)(2,1)} %copy-done.3) | copy-start | bytes 1990660
  237.6 129.6 %copy-start.2 = (bf16[3,3456,32]{1,2,0:T(8,128)(2,1)S(1)}, bf16[3,3456,32]{1,2,0:T(8,128)(2,1)}, u32[]{:S(2)}) copy-start(bf16[3,3456,32]{1,2,0:T(8,128)(2,1)} %copy-done.1) | copy-start | bytes 1990660
Sparse Core Ops, SparseCore 0:
  237.0 123.7 all-gather.3

commit v4 on v3

--- a/solution.py
+++ b/solution.py
@@ -57,13 +57,13 @@
     samples, here, chans = features.shape
     parts = lax.axis_size("rows")
     slice_width = chans // parts
-    blocks = jnp.transpose(features.reshape(samples, here, parts, slice_width), (2, 0, 1, 3))
+    blocks = jnp.transpose(features.reshape(samples, here, parts, slice_width), (2, 1, 0, 3))
     arrived = lax.all_to_all(blocks, "rows", split_axis=0, concat_axis=0, tiled=True)
-    chan_field = jnp.transpose(arrived, (1, 0, 2, 3)).reshape(samples, parts * here, slice_width)
+    chan_field = jnp.transpose(arrived, (2, 0, 1, 3)).reshape(samples, parts * here, slice_width)
     chan_mixed = depthwise(chan_field, depth_weight, 1).astype(jnp.bfloat16)
-    outgoing = jnp.transpose(chan_mixed.reshape(samples, parts, here, slice_width), (1, 0, 2, 3))
+    outgoing = jnp.transpose(chan_mixed.reshape(samples, parts, here, slice_width), (1, 2, 0, 3))
     returned = lax.all_to_all(outgoing, "rows", split_axis=0, concat_axis=0, tiled=True)
-    row_mixed = jnp.transpose(returned, (1, 2, 0, 3)).reshape(samples * here, chans)
+    row_mixed = jnp.transpose(returned, (2, 1, 0, 3)).reshape(samples * here, chans)
     pre = jnp.dot(row_mixed, point_weight, preferred_element_type=jnp.float32)
     act, pull = jax.vjp(gelu_tanh, pre)
     branch_out = act.astype(jnp.bfloat16).reshape(samples, here, K)

time: 407 us -> 407 us (level)
  no operation moved by 1% of the time
where the time goes in v4:
time: 407 us
  waiting for transfers between devices  282 us (69%)
  starting transfers between devices  34.2 us (8%)
  local copies, waits for them, and re-layouts  33 us (8%)
  blocking collectives  24.1 us (6%)
  between operations  14.2 us (3%)
  matrix products  12.2 us (3%)
  other arithmetic  7.17 us (2%)
    all_gather x1, waiting for transfers between devices, on_device(): lax.all_gather(grad_pre.reshape(samples, here, K), 'rows', axis=1, tiled=...  123 us
    all_to_all x1, waiting for transfers between devices, on_device(): lax.all_to_all(outgoing, 'rows', split_axis=0, concat_axis=0, tiled=True)  79.7 us
    all_to_all x1, waiting for transfers between devices, on_device(): lax.all_to_all(blocks, 'rows', split_axis=0, concat_axis=0, tiled=True)  78.8 us
    all_to_all x1, starting transfers between devices, on_device(): lax.all_to_all(blocks, 'rows', split_axis=0, concat_axis=0, tiled=True)  29.4 us
    all_gather x1, blocking collectives, on_device(): summed = lax.all_gather(packed, 'dp', axis=0, tiled=False).sum(axis=0)  24.1 us
    unnamed x19, local copies, waits for them, and re-layouts  15.4 us
  transfers between devices with their start and end apart: 3, of which 3 were waited for; matrix products, arithmetic and copies ran while one was open for 0% of the time, Pallas kernels for 0%

profile of v4, /device:TPU:2, one launch (start us, length us, event | category | flops | bytes accessed | tf_op | source)
XLA Modules:
  0.0 406.7 jit_solution(3015016212865202279)
XLA Ops:
  7.2 0.0 copy-start
  7.2 2.6 copy.12
  9.8 1.7 copy.31
  11.5 0.0 copy-start.6
  11.5 3.2 reshape.114
  14.7 29.4 %all-to-all-start = ((bf16[64,2,2592]{2,1,0:T(2,128)(2,1)}), bf16[64,2,2592]{2,1,0:T(2,128)(2,1)S(1)}, u32[]{:S(2)}, u32[]{:S(2)}) async-start(bf16[64,2,2592]{2,1,0:T(2,128)(2,1)} %reshape.114), calls=%async_computation | async-start | bytes 1376256 | tf_op jit(solution)/shard_map/all_to_all | solution.py:61
  44.2 0.0 copy-done.6
  44.2 78.8 %all-to-all-done = bf16[64,2,2592]{2,1,0:T(2,128)(2,1)S(1)} async-done(((bf16[64,2,2592]{2,1,0:T(2,128)(2,1)}), bf16[64,2,2592]{2,1,0:T(2,128)(2,1)S(1)}, u32[]{:S(2)}, u32[]{:S(2)}) %all-to-all-start) | async-done | bytes 663584 | tf_op jit(solution)/shard_map/all_to_all | solution.py:61
  123.0 3.1 reshape.115
  126.1 0.3 bitcast_bitcast_fusion.1
  126.4 0.6 copy.14
  127.0 2.1 reshape.93
  129.1 0.0 copy-start.3
  129.1 2.5 add_convert_fusion
  131.6 0.0 copy-start.1
  131.6 5.6 %reshape.94 = bf16[3,64,54,32]{2,1,3,0:T(8,128)(2,1)} reshape(bf16[3,3456,32]{1,2,0:T(8,128)(2,1)S(1)} %add_convert_fusion) | data formatting | bytes 1327104 | tf_op jit(solution)/shard_map/reshape | solution.py:64
  137.2 0.0 copy-done.3
  137.2 0.0 copy-done.1
  137.2 2.4 copy.30
  139.7 0.0 copy-start.5
  139.7 3.2 reshape.116
  142.9 4.8 %all-to-all-start.1 = ((bf16[64,2,2592]{2,1,0:T(2,128)(2,1)}), bf16[64,2,2592]{2,1,0:T(2,128)(2,1)S(1)}, u32[]{:S(2)}, u32[]{:S(2)}) async-start(bf16[64,2,2592]{2,1,0:T(2,128)(2,1)} %reshape.116), calls=%async_computation.1 | async-start | bytes 1376256 | tf_op jit(solution)/shard_map/all_to_all | solution.py:65
  147.8 0.0 all-gather.4.cloned.1.call-start
  147.8 0.0 copy-done.5
  147.8 79.7 %all-to-all-done.1 = bf16[64,2,2592]{2,1,0:T(2,128)(2,1)S(1)} async-done(((bf16[64,2,2592]{2,1,0:T(2,128)(2,1)}), bf16[64,2,2592]{2,1,0:T(2,128)(2,1)S(1)}, u32[]{:S(2)}, u32[]{:S(2)}) %all-to-all-start.1) | async-done | bytes 663584 | tf_op jit(solution)/shard_map/all_to_all | solution.py:65
  227.6 3.1 reshape.117
  230.7 0.3 bitcast_bitcast_fusion
  231.0 1.1 copy.16
  232.0 2.2 reshape.95
  234.2 0.0 copy-done
  234.3 0.0 copy-start.4
  234.3 1.9 fusion.28
  236.2 0.7 copy.17
  236.9 0.0 all-gather.4.cloned.1.call-update
  236.9 0.7 reshape.96
  237.6 0.0 copy-start.2
  237.6 123.2 %all-gather.4.cloned.1.call-done = bf16[3,3456,256]{2,0,1:T(4,128)(2,1)} async-done(((bf16[3,54,256]{2,0,1:T(4,128)(2,1)}), bf16[3,3456,256]{2,0,1:T(4,128)(2,1)}) %all-gather.4.cloned.1.call-update) | async-done | bytes 5308432 | tf_op jit(solution)/shard_map/all_gather | solution.py:71
  360.8 0.0 copy-done.4
  360.8 6.3 %fusion.18 = (f32[32]{0:T(128)S(1)}, f32[32]{0:T(128)S(1)}, f32[32]{0:T(128)S(1)}, f32[32]{0:T(128)S(1)}, f32[32]{0:T(128)S(1)}, /*index=5*/f32[32]{0:T(128)S(1)...) fusion(pred[3456]{0:T(1024)(128)(4,1)S(1)} %get-tuple-element.31, ...), kind=kOutput, calls=%fused_computation.45 | convolution fusion | flops 182476512 | bytes 6665348 | tf_op jit(solution)/shard_map/dot_general | solution.py:74
  367.1 0.0 copy-done.2
  367.1 4.0 fusion.19
  371.2 24.1 %all-gather.1 = f32[16,41,256]{2,1,0:T(8,128)S(1)} all-gather(f32[1,41,256]{2,1,0:T(8,128)S(1)} %fusion.29), channel_id=2, replica_groups=mesh['rows'=64,'dp'=16] {'dp'}, dimensions={0}, use_global_device_ids=true | all-gather | bytes 713728 | tf_op jit(solution)/shard_map/all_gather | solution.py:86
  395.3 0.1 reduce_sum.99
  395.4 0.6 slice_multiply_fusion
  396.0 0.6 slice_multiply_fusion.1
  396.6 3.3 fusion.9
  (7 shorter events, 0.2 us)
Async XLA Ops:
  7.2 227.1 %copy-start = (bf16[2048,256]{1,0:T(8,128)(2,1)S(1)}, bf16[2048,256]{1,0:T(8,128)(2,1)}, u32[]{:S(2)}) copy-start(bf16[2048,256]{1,0:T(8,128)(2,1)} %param.6) | copy-start | bytes 3145732
  11.5 32.7 %copy-start.6 = (bf16[9,32]{1,0:T(8,128)(2,1)S(1)}, bf16[9,32]{1,0:T(8,128)(2,1)}, u32[]{:S(2)}) copy-start(bf16[9,32]{1,0:T(8,128)(2,1)} %param.5) | copy-start | bytes 1732
  14.7 108.2 %all-to-all-start = ((bf16[64,2,2592]{2,1,0:T(2,128)(2,1)}), bf16[64,2,2592]{2,1,0:T(2,128)(2,1)S(1)}, u32[]{:S(2)}, u32[]{:S(2)}) async-start(bf16[64,2,2592]{2,1,0:T(2,128)(2,1)} %reshape.114), calls=%async_computation | async-start | bytes 1376256 | tf_op jit(solution)/shard_map/all_to_all | solution.py:61
  129.1 8.1 %copy-start.3 = (bf16[3,3456,32]{1,2,0:T(8,128)(2,1)}, bf16[3,3456,32]{1,2,0:T(8,128)(2,1)S(1)}, u32[]{:S(2)}) copy-start(bf16[3,3456,32]{1,2,0:T(8,128)(2,1)S(1)} %reshape.93) | copy-start | bytes 1990660
  131.6 5.6 %copy-start.1 = (bf16[3,3456,32]{1,2,0:T(8,128)(2,1)}, bf16[3,3456,32]{1,2,0:T(8,128)(2,1)S(1)}, u32[]{:S(2)}) copy-start(bf16[3,3456,32]{1,2,0:T(8,128)(2,1)S(1)} %add_convert_fusion) | copy-start | bytes 1990660
  139.7 8.1 %copy-start.5 = (bf16[3,54,256]{2,1,0:T(8,128)(2,1)S(1)}, bf16[3,54,256]{2,1,0:T(8,128)(2,1)}, u32[]{:S(2)}) copy-start(bf16[3,54,256]{2,1,0:T(8,128)(2,1)} %param.7) | copy-start | bytes 248836
  142.9 84.6 %all-to-all-start.1 = ((bf16[64,2,2592]{2,1,0:T(2,128)(2,1)}), bf16[64,2,2592]{2,1,0:T(2,128)(2,1)S(1)}, u32[]{:S(2)}, u32[]{:S(2)}) async-start(bf16[64,2,2592]{2,1,0:T(2,128)(2,1)} %reshape.116), calls=%async_computation.1 | async-start | bytes 1376256 | tf_op jit(solution)/shard_map/all_to_all | solution.py:65
  147.8 213.0 %all-gather.4.cloned.1.call-start = ((), (), s32[]{:S(2)}) async-start(), calls=%async_computation.2 | async-start | bytes 7188480 | tf_op jit(solution)/shard_map/all_gather | solution.py:71
  234.3 126.5 %copy-start.4 = (bf16[3,3456,32]{1,2,0:T(8,128)(2,1)S(1)}, bf16[3,3456,32]{1,2,0:T(8,128)(2,1)}, u32[]{:S(2)}) copy-start(bf16[3,3456,32]{1,2,0:T(8,128)(2,1)} %copy-done.3) | copy-start | bytes 1990660
  237.6 129.6 %copy-start.2 = (bf16[3,3456,32]{1,2,0:T(8,128)(2,1)S(1)}, bf16[3,3456,32]{1,2,0:T(8,128)(2,1)}, u32[]{:S(2)}) copy-start(bf16[3,3456,32]{1,2,0:T(8,128)(2,1)} %copy-done.1) | copy-start | bytes 1990660
Sparse Core Ops, SparseCore 0:
  237.0 123.7 all-gather.3
